TPU v7x, 32 devices: a whole 2x2x4 slice. The times are simulated.
32 devices in a mesh: chain: 2 (over x), ops: 8 (over z, y), sector: 2 (over core).
Axes of the slice: x: 2, y: 2, z: 4, core: 2. Of those that a mesh axis runs over, the one named last changes fastest.
Arguments:
- psi: bfloat16 [2, 8, 384, 384], P('chain', 'sector'), may hold values from -90 to 90
- left_ops: bfloat16 [2, 96, 8, 384, 384], P('chain', 'ops', 'sector'), may hold values from -1 to 2
- right_ops: bfloat16 [2, 96, 8, 384, 384], P('chain', 'ops', 'sector'), may hold values from -1 to 1
- basis: bfloat16 [2, 8, 384, 384], P('chain', 'sector'), may hold values from -0.3125 to 0.3125
- block_dims: int32 [2, 8], P('chain', 'sector'), may hold values from 64 to 384, as said below
Outputs:
- residual: float32 [2, 8, 384, 384], P('chain', 'sector', 'ops')
- thetas: float32 [2, 3], P('chain')
Inputs may be any that keep to these rules, and one draw needn't show every extreme that they name: `block_dims`: each is a multiple of 64; every section has a sector of exactly 384.
All inputs are finite; a program needn't handle non-finite values.
Results may differ from a plain program's by a relative error of at most 0.009.
Values may be sent and summed in bfloat16 or wider, within the bound.
No kernel may reach another device: no remote copies, remote signals or barrier semaphores. Data moves between devices by JAX's collectives and lax.ppermute only.
A program may use at most 128 MiB of HBM per device.

v0:
```python
import jax
import jax.numpy as jnp
from jax import lax
from jax.sharding import PartitionSpec as P

SECTORS = 8
ITERS = 3


def from_behind(block, axis, distance):
    devices = range(lax.axis_size(axis))
    route = [((i - distance) % len(devices), i) for i in devices]
    return lax.ppermute(block, axis, route)


def live_mask(block_dims, block_size):
    index_rows = jnp.arange(block_size, dtype=jnp.int32)
    limits = block_dims[:, :, None, None]
    inside = (index_rows[None, None, :, None] < limits) & (index_rows[None, None, None, :] < limits)
    return inside.astype(jnp.float32)


ROW_TILE = 64
LANE_TILE = 128
CLASSES = 8


def tile_counts(dims, block_size):
    rows = jnp.clip((dims + ROW_TILE - 1) // ROW_TILE, 0, block_size // ROW_TILE)
    cols = jnp.clip((dims + LANE_TILE - 1) // LANE_TILE, 0, block_size // LANE_TILE)
    return (rows, cols)


def tile_plan(dims, block_size):
    rows, cols = tile_counts(dims, block_size)
    row_ids = jnp.arange(block_size // ROW_TILE)[None, :, None]
    col_ids = jnp.arange(block_size // LANE_TILE)[None, None, :]
    needed = ((row_ids < rows[:, None, None]) & (col_ids < cols[:, None, None])).reshape(-1)
    total = needed.shape[0]
    place = jnp.cumsum(needed.astype(jnp.int32)) - 1
    ids = jnp.arange(total, dtype=jnp.int32)
    order = jnp.zeros(total, jnp.int32).at[jnp.where(needed, place, total)].set(ids, mode="drop")
    return (order, jnp.sum(needed.astype(jnp.int32)))


def size_classes(sectors, block_size):
    total = sectors * (block_size // ROW_TILE) * (block_size // LANE_TILE)
    return sorted({-(-k * total // CLASSES) for k in range(1, CLASSES + 1)})


def tile_index(order, size, block_size):
    per_row = block_size // LANE_TILE
    per_sector = block_size // ROW_TILE * per_row
    picked = order[:size]
    return (picked // per_sector, picked // per_row % (block_size // ROW_TILE), picked % per_row)


def tiled(array):
    block_size = array.shape[-1]
    return array.reshape(
        array.shape[:-2] + (block_size // ROW_TILE, ROW_TILE, block_size // LANE_TILE, LANE_TILE)
    )


def pack(array, order, size, lead):
    sector_ids, row_ids, col_ids = tile_index(order, size, array.shape[-1])
    where = (slice(None),) * lead + (sector_ids, row_ids, slice(None), col_ids, slice(None))
    return tiled(array)[where]


def unpack(packed, order, count, size, like, lead):
    sector_ids, row_ids, col_ids = tile_index(order, size, like.shape[-1])
    sector_ids = jnp.where(jnp.arange(size) < count, sector_ids, like.shape[lead])
    where = (slice(None),) * lead + (sector_ids, row_ids, slice(None), col_ids, slice(None))
    room = jnp.zeros(tiled(like).shape, packed.dtype)
    return room.at[where].set(packed, mode="drop").reshape(like.shape)


def class_index(block_dims, block_size, classes):
    every = lax.all_gather(block_dims[0], ("chain", "sector"))
    rows, cols = tile_counts(every, block_size)
    need = jnp.max(jnp.sum(rows * cols, axis=-1))
    return jnp.sum((jnp.asarray(classes, jnp.int32) < need).astype(jnp.int32))


def chain_move(env, send_order, recv_order, recv_count, choice, classes):

    def branch(size):

        def run(env, send_order, recv_order, recv_count):
            arrived = from_behind(pack(env, send_order, size, 2), "chain", 1)
            return unpack(arrived, recv_order, recv_count, size, env, 2)

        return run

    return lax.switch(choice, [branch(s) for s in classes], env, send_order, recv_order, recv_count)


def ops_sum(partial, order, count, choice, classes):

    def branch(size):

        def run(partial, order, count):
            summed = lax.psum(pack(partial, order, size, 1), "ops")
            return unpack(summed, order, count, size, partial, 1)

        return run

    return lax.switch(choice, [branch(s) for s in classes], partial, order, count)


def gather_sector(values):
    count = lax.axis_size("sector")
    slots = jnp.zeros((count, values.shape[0]), jnp.float32)
    slots = slots.at[lax.axis_index("sector")].set(values)
    return lax.psum(slots, "sector")


def quotient(vector_wide, sigma_full):
    norm_part = jnp.sum(vector_wide * vector_wide)
    corr_part = jnp.sum(vector_wide * sigma_full)
    local_theta = jnp.where(
        norm_part > 0, corr_part / jnp.where(norm_part > 0, norm_part, 1.0), 0.0
    )
    local_rest = sigma_full - local_theta * vector_wide
    rest_part = jnp.sum(local_rest * local_rest)
    cross_part = jnp.sum(vector_wide * local_rest)
    table = gather_sector(jnp.stack([norm_part, corr_part, rest_part, cross_part, local_theta]))
    norms, corrs, rests, crosses, thetas = (table[:, i] for i in range(5))
    rayleigh = jnp.sum(corrs) / jnp.sum(norms)
    shift = thetas - rayleigh
    spread = jnp.sum(rests + 2.0 * shift * crosses + shift * shift * norms)
    return (rayleigh, spread)


def on_device(psi, left_ops, right_ops, basis, block_dims):
    block_size = psi.shape[2]
    live = live_mask(block_dims, block_size)
    classes = size_classes(psi.shape[1], block_size)
    choice = class_index(block_dims, block_size, classes)
    own_order, own_count = tile_plan(block_dims[0], block_size)
    target_dims = from_behind(block_dims, "chain", -1)
    send_order, _ = tile_plan(target_dims[0], block_size)
    half_env = jnp.einsum(
        "ckqab,cqbd->ckqad", left_ops, basis, preferred_element_type=jnp.float32
    ).astype(jnp.bfloat16)
    boundary_ops = jnp.einsum(
        "cqba,ckqbd->ckqad", basis, half_env, preferred_element_type=jnp.float32
    ).astype(jnp.bfloat16)
    shifted = chain_move(boundary_ops, send_order, own_order, own_count, choice, classes)
    vector = jnp.where(live > 0, psi, jnp.zeros_like(psi))
    entry_count = float(SECTORS * block_size * block_size)
    share_rows = block_size // lax.axis_size("ops")
    row_start = lax.axis_index("ops") * share_rows
    residual = None
    quotients = []
    for iteration in range(ITERS):
        products = jnp.einsum(
            "ckqab,cqbd->ckqad", shifted, vector, preferred_element_type=jnp.float32
        ).astype(jnp.bfloat16)
        partial_sigma = jnp.einsum(
            "ckqad,ckqed->cqae", products, right_ops, preferred_element_type=jnp.float32
        )
        sigma_full = ops_sum(partial_sigma, own_order, own_count, choice, classes) * live
        vector_wide = vector.astype(jnp.float32)
        rayleigh, spread = quotient(vector_wide, sigma_full)
        quotients.append(rayleigh)
        residue = sigma_full - rayleigh * vector_wide
        if iteration + 1 < ITERS:
            vector = (residue * lax.rsqrt(spread / entry_count + 1e-06)).astype(jnp.bfloat16)
        else:
            residual = lax.dynamic_slice_in_dim(residue, row_start, share_rows, 2)
    thetas = jnp.stack(quotients).reshape(1, ITERS)
    return (residual, thetas)


def solution(mesh):
    in_specs = (
        P("chain", "sector", None, None),
        P("chain", "ops", "sector", None, None),
        P("chain", "ops", "sector", None, None),
        P("chain", "sector", None, None),
        P("chain", "sector"),
    )
    out_specs = (P("chain", "sector", "ops", None), P("chain", None))
    return jax.shard_map(
        on_device, mesh=mesh, in_specs=in_specs, out_specs=out_specs, check_vma=False
    )
```

profile of v0, /device:TPU:0, one launch (start us, length us, event | category | flops | bytes accessed | tf_op | source)
XLA Modules:
  0.0 997.5 jit_solution(8939563958995975156)
XLA Ops:
  7.2 3.0 collective-permute-start.8
  10.2 0.7 fusion.452
  11.3 0.7 convert_reduce_fusion
  12.2 5.2 all-gather
  17.3 1.3 iota_compare_fusion
  18.8 0.8 scatter_custom_fusion.32
  19.7 21.1 %convert_bitcast_fusion = bf16[1,12,4,384,384]{3,4,1,2,0:T(8,128)(2,1)} fusion(bf16[1,4,384,384]{3,2,1,0:T(8,128)(2,1)S(1)} %copy-done, bf16[1,12,4,384,384]{4,3,2,1,0:T(8,128)(2,1)} %param.45), kind=kOutput, calls=%fused_computation.911 | convolution fusion | flops 10885791744 | bytes 29491200 | tf_op jit(solution)/shard_map/cqba,ckqbd->ckqad/dot_general | solution.py:147
  41.5 1.3 fusion.448
  43.5 0.7 and_reduce_fusion
  45.0 0.8 scatter_custom_fusion.33
  45.8 438.7 %conditional.4 = (bf16[12,4,384,384]{3,2,0,1:T(8,128)(2,1)}) conditional(s32[]{:T(128)} %clamp.28, (s32[]{:T(128)}, s32[72]{0:T(128)S(1)}, bf16[1,12,4,384,384]{3,4,1,2,0:T(8,128)(2,1)}, s32[72]{0:T(128)S(1)}) %tuple.124, (s32[]{:T(128)}, s32[72]{0:T(128)S(1)}, bf16[1,12,4,384,384]{3,4,1,2,0:T(8,128)(2,1)}, ...), branch_computations={%region_8.10_spmd, %region_10.12_spmd, %region_12.14_spmd, %region... | conditional | flops 6480 | bytes 254806912 | solution.py:96
  56.0 42.8 %reshape.1812 = bf16[12,4,6,64,3,128]{3,2,5,4,0,1:T(8,128)(2,1)} reshape(bf16[1,12,4,384,384]{3,4,1,2,0:T(8,128)(2,1)} %get-tuple-element.537) | data formatting | bytes 28311552 | tf_op jit(solution)/shard_map/cond/branch_5_fun/reshape | solution.py:60
  98.8 34.4 %copy.314 = bf16[12,4,6,64,3,128]{5,3,4,2,1,0:T(8,128)(2,1)} copy(bf16[12,4,6,64,3,128]{3,2,5,4,0,1:T(8,128)(2,1)} %reshape.1812) | data formatting | bytes 28311552 | tf_op jit(solution)/shard_map/cond/branch_5_fun/reshape | solution.py:60
  133.3 12.7 %gather_fusion.5 = bf16[54,12,64,128]{3,2,1,0:T(8,128)(2,1)} fusion(bf16[12,4,6,64,3,128]{5,3,4,2,1,0:T(8,128)(2,1)} %copy.314, s32[54]{0:T(128)S(1)} %fusion.72), kind=kCustom, calls=%fused_computation.5 | custom fusion | bytes 21234312 | tf_op jit(solution)/shard_map/cond/branch_5_fun/gather | solution.py:68
  146.6 229.5 %collective-permute-done.5 = bf16[54,1,12,64,128]{4,3,2,0,1:T(8,128)(2,1)} collective-permute-done((bf16[54,1,12,64,128]{4,3,2,0,1:T(8,128)(2,1)}, bf16[54,1,12,64,128]{4,3,2,0,1:T(8,128)(2,1)}, u32[]{:S(2)}, u32[]{:S(2)}) %collective-permute-start.5) | collective-permute-done | bytes 10616864 | tf_op jit(solution)/shard_map/cond/branch_5_fun/ppermute | solution.py:13
  376.1 8.6 broadcast.2387
  384.8 29.5 %scatter_fusion.5 = bf16[12,4,6,64,3,128]{5,3,4,2,1,0:T(8,128)(2,1)} fusion(bf16[12,4,6,64,3,128]{5,3,4,2,1,0:T(8,128)(2,1)} %broadcast.2387, s32[54]{0:T(128)S(1)} %fusion.77, bf16[54,12,64,128]{3,2,1,0:T(8,128)(2,1)} %bitcast.35), kind=kCustom, calls=%fused_computation.37 | custom fusion | bytes 31851144 | tf_op jit(solution)/shard_map/cond/branch_5_fun/scatter | solution.py:76
  414.3 20.5 %copy.450 = bf16[12,4,6,64,3,128]{5,4,3,2,0,1:T(4,128)(2,1)} copy(bf16[12,4,6,64,3,128]{5,3,4,2,1,0:T(8,128)(2,1)} %scatter_fusion.5) | data formatting | bytes 28311552 | tf_op jit(solution)/shard_map/cond | solution.py:96
  434.8 35.9 %reshape.1820 = bf16[12,4,384,384]{3,2,0,1:T(8,128)(2,1)} reshape(bf16[12,4,6,64,3,128]{5,4,3,2,0,1:T(4,128)(2,1)} %copy.450) | data formatting | bytes 28311552 | tf_op jit(solution)/shard_map/cond | solution.py:96
  484.6 20.6 %fusion.415 = f32[1,4,384,384]{3,2,1,0:T(8,128)S(1)} fusion(bf16[12,4,384,384]{3,2,0,1:T(8,128)(2,1)} %get-tuple-element.547, bf16[1,4,384,384]{3,2,1,0:T(8,128)(2,1)S(1)} %copy-done.2, pred[4,384]{1,0:T(4,128)(4,1)S(1)} %copy-done.9, bf16[1,12,4,384,384]{4,3,2,1,0:T(8,128)(2,1)} %param.46), kind=kOutput, calls=%fused_computation.956 | convolution fusion | flops 10881073152 | bytes 31852032 | tf_op jit(solution)/shard_map/ckqad,ckqed->cqae/dot_general | solution.py:161
  505.3 135.6 %conditional.5 = (f32[1,4,384,384]{3,2,1,0:T(8,128)S(1)}) conditional(s32[]{:T(128)} %clamp.28, (s32[]{:T(128)}, s32[72]{0:T(128)S(1)}, f32[1,4,384,384]{3,2,1,0:T(8,128)S(1)}) %tuple.125, (s32[]{:T(128)}, s32[72]{0:T(128)S(1)}, f32[1,4,384,384]{3,2,1,0:T(8,128)S(1)}) %tuple.125, (s32[]{:T(128)}, s32[72]{0:T(128)S(1)}, ...), branch_computations={%region_24.27_spmd, %region_27.30_spmd, %region_30.33_spmd, %regio... | conditional | flops 595872 | bytes 47189432 | solution.py:109
  512.1 2.5 reshape.977
  514.6 2.2 copy.330
  516.8 2.4 gather_fusion.13
  519.8 98.0 %all-reduce.35.cloned.1.call-done = f32[54,1,64,128]{3,2,0,1:T(8,128)} async-done(((f32[54,1,64,128]{3,2,0,1:T(8,128)}), f32[54,1,64,128]{3,2,0,1:T(8,128)}) %all-reduce.35.cloned.1.call-update) | async-done | bytes 1769488 | tf_op jit(solution)/shard_map/cond/branch_5_fun/psum | solution.py:104
  618.2 7.9 scatter_fusion.13
  626.0 3.4 copy.331
  629.4 3.8 reshape.812
  640.9 2.0 fusion.401
  644.9 2.1 fusion.403
  646.9 2.7 stack.71
  650.3 2.5 psum.189
  652.8 0.7 slice_reduce_fusion.5
  656.2 2.1 fusion.406
  658.2 20.2 %fusion.420 = f32[1,4,384,384]{3,2,1,0:T(8,128)S(1)} fusion(bf16[12,4,384,384]{3,2,0,1:T(8,128)(2,1)} %get-tuple-element.547, bf16[1,4,384,384]{3,2,1,0:T(8,128)(2,1)S(1)} %fusion.406, bf16[1,12,4,384,384]{4,3,2,1,0:T(8,128)(2,1)} %param.46), kind=kOutput, calls=%fused_computation.957 | convolution fusion | flops 10878713856 | bytes 31850496 | tf_op jit(solution)/shard_map/ckqad,ckqed->cqae/dot_general | solution.py:161
  678.4 130.4 %conditional.6 = (f32[1,4,384,384]{3,2,1,0:T(8,128)S(1)}) conditional(s32[]{:T(128)} %clamp.28, (s32[]{:T(128)}, s32[72]{0:T(128)S(1)}, f32[1,4,384,384]{3,2,1,0:T(8,128)S(1)}) %tuple.126, (s32[]{:T(128)}, s32[72]{0:T(128)S(1)}, f32[1,4,384,384]{3,2,1,0:T(8,128)S(1)}) %tuple.126, (s32[]{:T(128)}, s32[72]{0:T(128)S(1)}, ...), branch_computations={%region_57.60_spmd, %region_60.63_spmd, %region_63.66_spmd, %regio... | conditional | flops 595872 | bytes 47189432 | solution.py:109
  685.2 2.5 reshape.1041
  687.7 2.2 copy.346
  689.9 2.4 gather_fusion.21
  693.0 92.6 %all-reduce.51.cloned.1.call-done = f32[54,1,64,128]{3,2,0,1:T(8,128)} async-done(((f32[54,1,64,128]{3,2,0,1:T(8,128)}), f32[54,1,64,128]{3,2,0,1:T(8,128)}) %all-reduce.51.cloned.1.call-update) | async-done | bytes 1769488 | tf_op jit(solution)/shard_map/cond/branch_5_fun/psum | solution.py:104
  785.8 7.9 scatter_fusion.21
  793.7 3.4 copy.347
  797.1 3.8 reshape.828
  808.8 1.7 fusion.408
  812.5 1.8 fusion.410
  814.4 2.7 stack.77
  817.7 2.5 psum.190
  820.2 0.7 slice_reduce_fusion.4
  823.6 2.5 fusion.459
  826.1 20.3 %fusion.425 = f32[1,4,384,384]{3,2,1,0:T(8,128)S(1)} fusion(bf16[12,4,384,384]{3,2,0,1:T(8,128)(2,1)} %get-tuple-element.547, bf16[1,4,384,384]{3,2,1,0:T(8,128)(2,1)} %get-tuple-element.616, bf16[1,12,4,384,384]{4,3,2,1,0:T(8,128)(2,1)} %param.46), kind=kOutput, calls=%fused_computation.958 | convolution fusion | flops 10878713856 | bytes 31850496 | tf_op jit(solution)/shard_map/ckqad,ckqed->cqae/dot_general | solution.py:161
  846.4 124.8 %conditional.7 = (f32[1,4,384,384]{3,2,1,0:T(8,128)S(1)}) conditional(s32[]{:T(128)} %clamp.28, (s32[]{:T(128)}, s32[72]{0:T(128)S(1)}, f32[1,4,384,384]{3,2,1,0:T(8,128)S(1)}) %tuple.127, (s32[]{:T(128)}, s32[72]{0:T(128)S(1)}, f32[1,4,384,384]{3,2,1,0:T(8,128)S(1)}) %tuple.127, (s32[]{:T(128)}, s32[72]{0:T(128)S(1)}, ...), branch_computations={%region_89.92_spmd, %region_92.95_spmd, %region_95.98_spmd, %regio... | conditional | flops 595872 | bytes 47189432 | solution.py:109
  853.2 2.5 reshape.1105
  855.7 2.2 copy.362
  857.9 2.4 gather_fusion.29
  861.0 92.6 %all-reduce.67.cloned.1.call-done = f32[54,1,64,128]{3,2,0,1:T(8,128)} async-done(((f32[54,1,64,128]{3,2,0,1:T(8,128)}), f32[54,1,64,128]{3,2,0,1:T(8,128)}) %all-reduce.67.cloned.1.call-update) | async-done | bytes 1769488 | tf_op jit(solution)/shard_map/cond/branch_5_fun/psum | solution.py:104
  953.9 7.9 scatter_fusion.29
  961.7 3.4 copy.363
  965.1 3.8 reshape.844
  971.2 1.4 copy-done.3
  972.6 3.2 multiply_reduce_fusion.2
  977.7 2.6 multiply_reduce_fusion
  980.3 2.7 stack.83
  983.6 2.5 psum.191
  988.1 1.7 dynamic-slice_subtract_fusion
  (72 shorter events, 10.3 us)
Async XLA Ops:
  7.2 12.5 %copy-start = (bf16[1,4,384,384]{3,2,1,0:T(8,128)(2,1)S(1)}, bf16[1,4,384,384]{3,2,1,0:T(8,128)(2,1)}, u32[]{:S(2)}) copy-start(bf16[1,4,384,384]{3,2,1,0:T(8,128)(2,1)} %param.47) | copy-start | bytes 3538948
  7.2 37.0 %collective-permute-start.8 = (s32[1,4]{1,0:T(1,128)}, s32[1,4]{1,0:T(1,128)S(1)}, u32[]{:S(2)}, u32[]{:S(2)}) collective-permute-start(s32[1,4]{1,0:T(1,128)} %param.48), channel_id=1, source_target_pairs={{16,0},{0,16},{17,1},{1,17},{18,2},{2,18},{19,3},{3,19},{20,4},{4,... | collective-permute-start | bytes 56 | tf_op jit(solution)/shard_map/ppermute | solution.py:13
  19.7 21.9 %copy-start.12 = (s32[8]{0:T(128)S(1)}, s32[8]{0:T(128)}, u32[]{:S(2)}) copy-start(s32[8]{0:T(128)} %constant.1748.clone) | copy-start | bytes 100
  19.7 23.8 %copy-start.11 = (s32[2]{0:T(128)S(1)}, s32[2]{0:T(128)}, u32[]{:S(2)}) copy-start(s32[2]{0:T(128)} %constant.1739.clone.1) | copy-start | bytes 28
  45.8 438.8 %copy-start.2 = (bf16[1,4,384,384]{3,2,1,0:T(8,128)(2,1)S(1)}, bf16[1,4,384,384]{3,2,1,0:T(8,128)(2,1)}, u32[]{:S(2)}) copy-start(bf16[1,4,384,384]{3,2,1,0:T(8,128)(2,1)} %param.44) | copy-start | bytes 3538948
  45.8 438.8 %copy-start.9 = (pred[4,384]{1,0:T(4,128)(4,1)S(1)}, pred[4,384]{1,0:T(4,128)(4,1)}, u32[]{:S(2)}) copy-start(pred[4,384]{1,0:T(4,128)(4,1)} %iota_compare_fusion) | copy-start | bytes 4612
  146.0 230.1 %collective-permute-start.5 = (bf16[54,1,12,64,128]{4,3,2,0,1:T(8,128)(2,1)}, bf16[54,1,12,64,128]{4,3,2,0,1:T(8,128)(2,1)}, u32[]{:S(2)}, u32[]{:S(2)}) collective-permute-start(bf16[54,1,12,64,128]{4,3,2,0,1:T(8,128)(2,1)} %bitcast.1130), channel_id=1, source_target_pairs={{16,0},{0,16},{17,1},{1,17},{18,2},{2,18},{19,3},{3,19},{20,4},{4,... | collective-permute-start | bytes 31850504 | tf_op jit(solution)/shard_map/cond/branch_5_fun/ppermute | solution.py:13
  512.0 105.9 %all-reduce.35.cloned.1.call-start = ((), (), s32[]{:S(2)}) async-start(), calls=%async_computation.5 | async-start | bytes 3538944 | tf_op jit(solution)/shard_map/cond/branch_5_fun/psum | solution.py:104
  685.1 100.4 %all-reduce.51.cloned.1.call-start = ((), (), s32[]{:S(2)}) async-start(), calls=%async_computation.13 | async-start | bytes 3538944 | tf_op jit(solution)/shard_map/cond/branch_5_fun/psum | solution.py:104
  853.1 100.5 %all-reduce.67.cloned.1.call-start = ((), (), s32[]{:S(2)}) async-start(), calls=%async_computation.21 | async-start | bytes 3538944 | tf_op jit(solution)/shard_map/cond/branch_5_fun/psum | solution.py:104
  971.2 1.4 copy-start.3
  972.6 17.8 %copy-start.1 = (bf16[1,4,384,384]{3,2,1,0:T(8,128)(2,1)S(1)}, bf16[1,4,384,384]{3,2,1,0:T(8,128)(2,1)}, u32[]{:S(2)}) copy-start(bf16[1,4,384,384]{3,2,1,0:T(8,128)(2,1)} %param.47) | copy-start | bytes 3538948
Sparse Core Ops, SparseCore 0:
  519.3 98.4 all-reduce.34
  692.5 93.0 all-reduce.50
  860.5 93.0 all-reduce.66
where the time goes:
time: 1010 us; the launch traced here: 997 us
  waiting for transfers between devices  513 us (51%)
  local copies, waits for them, and re-layouts  264 us (26%)
  matrix products  82.1 us (8%)
  loops' own time  62 us (6%)
  other arithmetic  34 us (3%)
  between operations  26.7 us (3%)
  blocking collectives  12.6 us (1%)
    psum x3, waiting for transfers between devices, run(): summed = lax.psum(pack(partial, order, size, 1), 'ops')  283 us
    ppermute x2, waiting for transfers between devices, from_behind(): return lax.ppermute(block, axis, route)  230 us
    reshape x8, local copies, waits for them, and re-layouts, tiled(): array.reshape(array.shape[:-2] + (block_size // ROW_TILE, ROW_TILE, block...  91.4 us
    scatter x7, local copies, waits for them, and re-layouts, unpack(): return room.at[where].set(packed, mode='drop').reshape(like.shape)  63.3 us
    dot_general x3, matrix products, on_device(): jnp.einsum('ckqad,ckqed->cqae', products, right_ops, preferred_element_ty...  61.1 us
    cond x2, local copies, waits for them, and re-layouts, chain_move(): lax.switch(choice, [branch(s) for s in classes], env, send_order, recv_or...  56.5 us
    another operation x3, loops' own time, ops_sum(): lax.switch(choice, [branch(s) for s in classes], partial, order, count)  37.9 us
    another operation x1, loops' own time, chain_move(): lax.switch(choice, [branch(s) for s in classes], env, send_order, recv_or...  24.1 us
  transfers between devices with their start and end apart: 5, of which 4 were waited for; matrix products, arithmetic and copies ran while one was open for 3% of the time, Pallas kernels for 0%

commit v1 on v0

--- a/solution.py
+++ b/solution.py
@@ -101,7 +101,7 @@
     def branch(size):
 
         def run(partial, order, count):
-            summed = lax.psum(pack(partial, order, size, 1), "ops")
+            summed = lax.all_gather(pack(partial, order, size, 1), axis_name="ops").sum(axis=0)
             return unpack(summed, order, count, size, partial, 1)
 
         return run

time: 1010 us -> 1360 us (1.35)
  waiting for transfers between devices: 513 us -> 816 us
  other arithmetic: 34 us -> 57.7 us
  starting transfers between devices: 3.13 us -> 18.2 us
    all_gather x0 -> x3, waiting for transfers between devices: none -> 587 us  [run(): lax.all_gather(pack(partial, order, size, 1), axis_name='ops').sum(axis=0)]
    psum x3 -> x0, waiting for transfers between devices: 283 us -> none  [run(): summed = lax.psum(pack(partial, order, size, 1), 'ops')]
    reduce_sum x0 -> x3, other arithmetic: none -> 24.2 us  [run(): lax.all_gather(pack(partial, order, size, 1), axis_name='ops').sum(axis=0)]
    all_gather x0 -> x3, starting transfers between devices: none -> 15.2 us  [run(): lax.all_gather(pack(partial, order, size, 1), axis_name='ops').sum(axis=0)]
  transfers between devices with their start and end apart: 5 -> 5, of which waited for: 4 -> 4; matrix products, arithmetic and copies ran while one was open for 3% -> 2% of each run, Pallas kernels for 0% -> 0%
where the time goes in v1:
time: 1360 us; the launch traced here: 1350 us
  waiting for transfers between devices  816 us (60%)
  local copies, waits for them, and re-layouts  264 us (19%)
  matrix products  82.1 us (6%)
  loops' own time  72.3 us (5%)
  other arithmetic  57.7 us (4%)
  between operations  25.9 us (2%)
  starting transfers between devices  18.2 us (1%)
    all_gather x3, waiting for transfers between devices, run(): lax.all_gather(pack(partial, order, size, 1), axis_name='ops').sum(axis=0)  587 us
    ppermute x2, waiting for transfers between devices, from_behind(): return lax.ppermute(block, axis, route)  230 us
    reshape x8, local copies, waits for them, and re-layouts, tiled(): array.reshape(array.shape[:-2] + (block_size // ROW_TILE, ROW_TILE, block...  91.4 us
    scatter x7, local copies, waits for them, and re-layouts, unpack(): return room.at[where].set(packed, mode='drop').reshape(like.shape)  63.3 us
    dot_general x3, matrix products, on_device(): jnp.einsum('ckqad,ckqed->cqae', products, right_ops, preferred_element_ty...  61.1 us
    cond x2, local copies, waits for them, and re-layouts, chain_move(): lax.switch(choice, [branch(s) for s in classes], env, send_order, recv_or...  56.5 us
    another operation x3, loops' own time, ops_sum(): lax.switch(choice, [branch(s) for s in classes], partial, order, count)  50.5 us
  transfers between devices with their start and end apart: 5, of which 4 were waited for; matrix products, arithmetic and copies ran while one was open for 2% of the time, Pallas kernels for 0%

profile of v1, /device:TPU:0, one launch (start us, length us, event | category | flops | bytes accessed | tf_op | source)
XLA Modules:
  0.0 1348.9 jit_solution(8335729926075792634)
XLA Ops:
  7.2 3.0 collective-permute-start.8
  12.2 5.2 all-gather.24
  17.3 1.3 iota_compare_fusion
  18.8 0.8 scatter_custom_fusion.32
  19.7 21.1 %convert_bitcast_fusion = bf16[1,12,4,384,384]{3,4,1,2,0:T(8,128)(2,1)} fusion(bf16[1,4,384,384]{3,2,1,0:T(8,128)(2,1)S(1)} %copy-done, bf16[1,12,4,384,384]{4,3,2,1,0:T(8,128)(2,1)} %param.45), kind=kOutput, calls=%fused_computation.911 | convolution fusion | flops 10885791744 | bytes 29491200 | tf_op jit(solution)/shard_map/cqba,ckqbd->ckqad/dot_general | solution.py:147
  41.5 1.3 fusion.448
  45.8 436.5 %conditional.4 = (bf16[12,4,384,384]{3,2,0,1:T(8,128)(2,1)}) conditional(s32[]{:T(128)} %clamp.28, (s32[]{:T(128)}, s32[72]{0:T(128)S(1)}, bf16[1,12,4,384,384]{3,4,1,2,0:T(8,128)(2,1)}, s32[72]{0:T(128)S(1)}) %tuple.124, (s32[]{:T(128)}, s32[72]{0:T(128)S(1)}, bf16[1,12,4,384,384]{3,4,1,2,0:T(8,128)(2,1)}, ...), branch_computations={%region_8.10_spmd, %region_10.12_spmd, %region_12.14_spmd, %region... | conditional | flops 6480 | bytes 254806912 | solution.py:96
  56.4 42.8 %reshape.1908 = bf16[12,4,6,64,3,128]{3,2,5,4,0,1:T(8,128)(2,1)} reshape(bf16[1,12,4,384,384]{3,4,1,2,0:T(8,128)(2,1)} %get-tuple-element.537) | data formatting | bytes 28311552 | tf_op jit(solution)/shard_map/cond/branch_5_fun/reshape | solution.py:60
  99.1 34.4 %copy.314 = bf16[12,4,6,64,3,128]{5,3,4,2,1,0:T(8,128)(2,1)} copy(bf16[12,4,6,64,3,128]{3,2,5,4,0,1:T(8,128)(2,1)} %reshape.1908) | data formatting | bytes 28311552 | tf_op jit(solution)/shard_map/cond/branch_5_fun/reshape | solution.py:60
  133.6 12.7 gather_fusion.5
  146.9 229.5 %collective-permute-done.5 = bf16[54,1,12,64,128]{4,3,2,0,1:T(8,128)(2,1)} collective-permute-done((bf16[54,1,12,64,128]{4,3,2,0,1:T(8,128)(2,1)}, bf16[54,1,12,64,128]{4,3,2,0,1:T(8,128)(2,1)}, u32[]{:S(2)}, u32[]{:S(2)}) %collective-permute-start.5) | collective-permute-done | bytes 10616864 | tf_op jit(solution)/shard_map/cond/branch_5_fun/ppermute | solution.py:13
  376.5 8.6 broadcast.2387
  385.1 29.5 %scatter_fusion.5 = bf16[12,4,6,64,3,128]{5,3,4,2,1,0:T(8,128)(2,1)} fusion(bf16[12,4,6,64,3,128]{5,3,4,2,1,0:T(8,128)(2,1)} %broadcast.2387, s32[54]{0:T(128)S(1)} %fusion.77, bf16[54,12,64,128]{3,2,1,0:T(8,128)(2,1)} %bitcast.35), kind=kCustom, calls=%fused_computation.37 | custom fusion | bytes 31851144 | tf_op jit(solution)/shard_map/cond/branch_5_fun/scatter | solution.py:76
  414.6 20.5 %copy.450 = bf16[12,4,6,64,3,128]{5,4,3,2,0,1:T(4,128)(2,1)} copy(bf16[12,4,6,64,3,128]{5,3,4,2,1,0:T(8,128)(2,1)} %scatter_fusion.5) | data formatting | bytes 28311552 | tf_op jit(solution)/shard_map/cond | solution.py:96
  435.1 35.9 %reshape.1916 = bf16[12,4,384,384]{3,2,0,1:T(8,128)(2,1)} reshape(bf16[12,4,6,64,3,128]{5,4,3,2,0,1:T(4,128)(2,1)} %copy.450) | data formatting | bytes 28311552 | tf_op jit(solution)/shard_map/cond | solution.py:96
  482.3 20.6 %fusion.415 = f32[1,4,384,384]{3,2,1,0:T(8,128)S(1)} fusion(bf16[12,4,384,384]{3,2,0,1:T(8,128)(2,1)} %get-tuple-element.547, bf16[1,4,384,384]{3,2,1,0:T(8,128)(2,1)S(1)} %copy-done.2, pred[4,384]{1,0:T(4,128)(4,1)S(1)} %copy-done.6, bf16[1,12,4,384,384]{4,3,2,1,0:T(8,128)(2,1)} %param.46), kind=kOutput, calls=%fused_computation.956 | convolution fusion | flops 10881073152 | bytes 31852032 | tf_op jit(solution)/shard_map/ckqad,ckqed->cqae/dot_general | solution.py:161
  503.0 255.0 %conditional.5 = (f32[1,4,384,384]{3,2,1,0:T(8,128)S(1)}) conditional(s32[]{:T(128)} %clamp.28, (s32[]{:T(128)}, s32[72]{0:T(128)S(1)}, f32[1,4,384,384]{3,2,1,0:T(8,128)S(1)}) %tuple.125, (s32[]{:T(128)}, s32[72]{0:T(128)S(1)}, f32[1,4,384,384]{3,2,1,0:T(8,128)S(1)}) %tuple.125, (s32[]{:T(128)}, s32[72]{0:T(128)S(1)}, ...), branch_computations={%region_24.27_spmd, %region_27.30_spmd, %region_30.33_spmd, %regio... | conditional | flops 4134816 | bytes 117968312 | solution.py:109
  508.1 4.9 all-gather.60.cloned.1.call-start
  513.1 2.5 reshape.1001
  515.6 2.2 copy.330
  517.9 2.4 gather_fusion.13
  520.9 200.2 %all-gather.60.cloned.1.call-done = f32[432,64,128]{2,1,0:T(8,128)} async-done(((f32[54,64,128]{2,1,0:T(8,128)}), f32[432,64,128]{2,1,0:T(8,128)}) %all-gather.60.cloned.1.call-update) | async-done | bytes 14155792 | tf_op jit(solution)/shard_map/cond/branch_5_fun/all_gather | solution.py:104
  721.0 8.1 reduce.49
  729.4 7.9 scatter_fusion.13
  737.2 3.4 copy.331
  740.6 3.8 reshape.836
  758.0 2.0 fusion.401
  762.0 2.1 fusion.403
  764.1 2.7 stack.71
  767.5 2.5 psum.21
  773.1 2.1 fusion.406
  775.2 20.2 %fusion.420 = f32[1,4,384,384]{3,2,1,0:T(8,128)S(1)} fusion(bf16[12,4,384,384]{3,2,0,1:T(8,128)(2,1)} %get-tuple-element.547, bf16[1,4,384,384]{3,2,1,0:T(8,128)(2,1)S(1)} %fusion.406, bf16[1,12,4,384,384]{4,3,2,1,0:T(8,128)(2,1)} %param.46), kind=kOutput, calls=%fused_computation.957 | convolution fusion | flops 10878713856 | bytes 31850496 | tf_op jit(solution)/shard_map/ckqad,ckqed->cqae/dot_general | solution.py:161
  795.4 248.4 %conditional.6 = (f32[1,4,384,384]{3,2,1,0:T(8,128)S(1)}) conditional(s32[]{:T(128)} %clamp.28, (s32[]{:T(128)}, s32[72]{0:T(128)S(1)}, f32[1,4,384,384]{3,2,1,0:T(8,128)S(1)}) %tuple.126, (s32[]{:T(128)}, s32[72]{0:T(128)S(1)}, f32[1,4,384,384]{3,2,1,0:T(8,128)S(1)}) %tuple.126, (s32[]{:T(128)}, s32[72]{0:T(128)S(1)}, ...), branch_computations={%region_57.60_spmd, %region_60.63_spmd, %region_63.66_spmd, %regio... | conditional | flops 4134816 | bytes 117968312 | solution.py:109
  800.3 5.0 all-gather.76.cloned.1.call-start
  805.3 2.5 reshape.1065
  807.9 2.2 copy.346
  810.1 2.4 gather_fusion.21
  813.1 193.3 %all-gather.76.cloned.1.call-done = f32[432,64,128]{2,1,0:T(8,128)} async-done(((f32[54,64,128]{2,1,0:T(8,128)}), f32[432,64,128]{2,1,0:T(8,128)}) %all-gather.76.cloned.1.call-update) | async-done | bytes 14155792 | tf_op jit(solution)/shard_map/cond/branch_5_fun/all_gather | solution.py:104
  1006.4 8.1 reduce.57
  1014.8 7.9 scatter_fusion.21
  1022.6 3.4 copy.347
  1026.1 3.8 reshape.852
  1043.8 1.6 fusion.408
  1047.2 1.8 fusion.410
  1048.9 2.5 stack.77
  1052.1 2.5 psum.22
  1057.8 2.4 fusion.459
  1060.2 20.3 %fusion.425 = f32[1,4,384,384]{3,2,1,0:T(8,128)S(1)} fusion(bf16[12,4,384,384]{3,2,0,1:T(8,128)(2,1)} %get-tuple-element.547, bf16[1,4,384,384]{3,2,1,0:T(8,128)(2,1)} %get-tuple-element.616, bf16[1,12,4,384,384]{4,3,2,1,0:T(8,128)(2,1)} %param.46), kind=kOutput, calls=%fused_computation.958 | convolution fusion | flops 10878713856 | bytes 31850496 | tf_op jit(solution)/shard_map/ckqad,ckqed->cqae/dot_general | solution.py:161
  1080.4 242.7 %conditional.7 = (f32[1,4,384,384]{3,2,1,0:T(8,128)S(1)}) conditional(s32[]{:T(128)} %clamp.28, (s32[]{:T(128)}, s32[72]{0:T(128)S(1)}, f32[1,4,384,384]{3,2,1,0:T(8,128)S(1)}) %tuple.127, (s32[]{:T(128)}, s32[72]{0:T(128)S(1)}, f32[1,4,384,384]{3,2,1,0:T(8,128)S(1)}) %tuple.127, (s32[]{:T(128)}, s32[72]{0:T(128)S(1)}, ...), branch_computations={%region_89.92_spmd, %region_92.95_spmd, %region_95.98_spmd, %regio... | conditional | flops 4134816 | bytes 117968312 | solution.py:109
  1085.4 5.3 all-gather.92.cloned.1.call-start
  1090.7 2.5 reshape.1129
  1093.2 2.2 copy.362
  1095.4 2.4 gather_fusion.29
  1098.4 193.3 %all-gather.92.cloned.1.call-done = f32[432,64,128]{2,1,0:T(8,128)} async-done(((f32[54,64,128]{2,1,0:T(8,128)}), f32[432,64,128]{2,1,0:T(8,128)}) %all-gather.92.cloned.1.call-update) | async-done | bytes 14155792 | tf_op jit(solution)/shard_map/cond/branch_5_fun/all_gather | solution.py:104
  1291.7 8.1 reduce.65
  1300.1 7.9 scatter_fusion.29
  1308.0 3.4 copy.363
  1311.4 3.8 reshape.868
  1323.1 1.4 copy-done.3
  1324.5 3.2 multiply_reduce_fusion.2
  1329.7 2.5 multiply_reduce_fusion
  1332.1 2.6 stack.83
  1335.4 2.5 psum.23
  1339.8 1.7 dynamic-slice_subtract_fusion
  (75 shorter events, 14.3 us)
Async XLA Ops:
  7.2 12.5 copy-start
  7.2 37.0 %collective-permute-start.8 = (s32[1,4]{1,0:T(1,128)}, s32[1,4]{1,0:T(1,128)S(1)}, u32[]{:S(2)}, u32[]{:S(2)}) collective-permute-start(s32[1,4]{1,0:T(1,128)} %param.48), channel_id=1, source_target_pairs={{16,0},{0,16},{17,1},{1,17},{18,2},{2,18},{19,3},{3,19},{20,4},{4,... | collective-permute-start | bytes 56 | tf_op jit(solution)/shard_map/ppermute | solution.py:13
  19.7 21.9 %copy-start.8 = (s32[8]{0:T(128)S(1)}, s32[8]{0:T(128)}, u32[]{:S(2)}) copy-start(s32[8]{0:T(128)} %constant.1772.clone) | copy-start | bytes 100
  19.7 23.8 %copy-start.7 = (s32[2]{0:T(128)S(1)}, s32[2]{0:T(128)}, u32[]{:S(2)}) copy-start(s32[2]{0:T(128)} %constant.1763.clone.1) | copy-start | bytes 28
  45.8 436.5 %copy-start.2 = (bf16[1,4,384,384]{3,2,1,0:T(8,128)(2,1)S(1)}, bf16[1,4,384,384]{3,2,1,0:T(8,128)(2,1)}, u32[]{:S(2)}) copy-start(bf16[1,4,384,384]{3,2,1,0:T(8,128)(2,1)} %param.44) | copy-start | bytes 3538948
  45.8 436.5 %copy-start.6 = (pred[4,384]{1,0:T(4,128)(4,1)S(1)}, pred[4,384]{1,0:T(4,128)(4,1)}, u32[]{:S(2)}) copy-start(pred[4,384]{1,0:T(4,128)(4,1)} %iota_compare_fusion) | copy-start | bytes 4612
  146.3 230.2 %collective-permute-start.5 = (bf16[54,1,12,64,128]{4,3,2,0,1:T(8,128)(2,1)}, bf16[54,1,12,64,128]{4,3,2,0,1:T(8,128)(2,1)}, u32[]{:S(2)}, u32[]{:S(2)}) collective-permute-start(bf16[54,1,12,64,128]{4,3,2,0,1:T(8,128)(2,1)} %bitcast.1118), channel_id=1, source_target_pairs={{16,0},{0,16},{17,1},{1,17},{18,2},{2,18},{19,3},{3,19},{20,4},{4,... | collective-permute-start | bytes 31850504 | tf_op jit(solution)/shard_map/cond/branch_5_fun/ppermute | solution.py:13
  508.1 212.9 %all-gather.60.cloned.1.call-start = ((), (), s32[]{:S(2)}) async-start(), calls=%async_computation.5 | async-start | bytes 15925248 | tf_op jit(solution)/shard_map/cond/branch_5_fun/all_gather | solution.py:104
  800.3 206.1 %all-gather.76.cloned.1.call-start = ((), (), s32[]{:S(2)}) async-start(), calls=%async_computation.13 | async-start | bytes 15925248 | tf_op jit(solution)/shard_map/cond/branch_5_fun/all_gather | solution.py:104
  1085.4 206.4 %all-gather.92.cloned.1.call-start = ((), (), s32[]{:S(2)}) async-start(), calls=%async_computation.21 | async-start | bytes 15925248 | tf_op jit(solution)/shard_map/cond/branch_5_fun/all_gather | solution.py:104
  1323.1 1.4 copy-start.3
  1324.5 17.6 %copy-start.1 = (bf16[1,4,384,384]{3,2,1,0:T(8,128)(2,1)S(1)}, bf16[1,4,384,384]{3,2,1,0:T(8,128)(2,1)}, u32[]{:S(2)}) copy-start(bf16[1,4,384,384]{3,2,1,0:T(8,128)(2,1)} %param.47) | copy-start | bytes 3538948
Sparse Core Ops, SparseCore 0:
  520.4 200.5 all-gather.59
  812.6 193.7 all-gather.75
  1097.9 193.7 all-gather.91
